TPU v7x, 32 devices: a whole 2x2x4 slice. The times are simulated.
32 devices in a mesh: row: 8 (over z, core), col: 4 (over y, x).
Axes of the slice: x: 2, y: 2, z: 4, core: 2. Of those that a mesh axis runs over, the one named last changes fastest.
Arguments:
- demand: float32 [2048, 4096], P('row', 'col'), may hold values from 0.2 to 2
- leakage: float32 [2048, 4096], P('row', 'col'), may hold values from 0.05 to 0.5
- conductance: float32 [2048, 4096], P('row', 'col'), may hold values from 0.5 to 4
- vias: int32 [2048, 4096], P('row', 'col'), may hold values 0 or 1
- layer_of: int32 [256, 512], P('row'), may hold values from 0 to 31
- lateral_k: float32 [32, 256, 512], P('col', 'row'), may hold values from 0.3 to 3
- vertical_k: float32 [32, 256, 512], P('col', 'row'), may hold values from 0.1 to 1
Outputs:
- drop: float32 [2048, 4096], P('row', 'col')
- temperature: float32 [32, 256, 512], P('col', 'row')
All inputs are finite; a program needn't handle non-finite values. No bound on the sum of `vias` on one device may be relied on, other than what follows from the above.
Results may differ from a plain program's by a relative error of at most 0.0001.
Values sent between devices are 32-bit elements; how exact they have to be, the bound alone decides.
No kernel may reach another device: no remote copies, remote signals or barrier semaphores. Data moves between devices by JAX's collectives and lax.ppermute only.
A program may use at most 128 MiB of HBM per device.

v0:
```python
import jax
import jax.numpy as jnp
from jax import lax
from jax.sharding import PartitionSpec as P

COARSE = 8
SWEEPS = 4
HEAT_SWEEPS = 4
OUTER = 2


COND_SLOPE = 0.5
LEAK_SLOPE = 0.7
VIA_CONDUCT = 4.0

HALO = 4


def extended(block, sides, width):
    for axis, dim in sides:
        count = lax.axis_size(axis)
        forward = [(i, i + 1) for i in range(count - 1)]
        backward = [(target, source) for source, target in forward]
        low = lax.ppermute(
            lax.slice_in_dim(block, block.shape[dim] - width, None, axis=dim), axis, forward
        )
        high = lax.ppermute(lax.slice_in_dim(block, 0, width, axis=dim), axis, backward)
        block = jnp.concatenate([low, block, high], axis=dim)
    return block


def spread_cols(coarse, fine_cols):
    n = coarse.shape[1]
    ids = jnp.arange(fine_cols, dtype=jnp.int32) // COARSE
    onehot = (jnp.arange(n, dtype=jnp.int32)[:, None] == ids[None, :]).astype(jnp.float32)
    return jnp.dot(coarse, onehot, precision=lax.Precision.HIGHEST)


def fine_of(coarse, fine_cols):
    wide = spread_cols(coarse, fine_cols)
    rows = wide.shape[0]
    return jnp.broadcast_to(wide[:, None, :], (rows, COARSE, fine_cols)).reshape(rows * COARSE, fine_cols)


def coarse_of(fine):
    rows, cols = fine.shape
    summed_rows = jnp.sum(fine.reshape(rows // COARSE, COARSE, cols), axis=1)
    n = cols // COARSE
    ids = jnp.arange(cols, dtype=jnp.int32) // COARSE
    onehot = (ids[:, None] == jnp.arange(n, dtype=jnp.int32)[None, :]).astype(jnp.float32)
    return jnp.dot(summed_rows, onehot, precision=lax.Precision.HIGHEST) * (1.0 / (COARSE * COARSE))


def power_sweeps(drop_ext, cond_ext, load_ext, via_ext, inside):
    h = HALO
    c = cond_ext[1:-1, 1:-1]
    w_north = (c + cond_ext[:-2, 1:-1]) * 0.5
    w_south = (c + cond_ext[2:, 1:-1]) * 0.5
    w_west = (c + cond_ext[1:-1, :-2]) * 0.5
    w_east = (c + cond_ext[1:-1, 2:]) * 0.5
    denom = w_north + w_south + w_west + w_east + via_ext[1:-1, 1:-1]
    load = load_ext[1:-1, 1:-1]
    mask = inside[1:-1, 1:-1]
    d = drop_ext
    for s in range(SWEEPS):
        o = s
        e = denom.shape[0] - s
        f = denom.shape[1] - s
        sl = lambda a: a[o:e, o:f]
        summed = (
            sl(load)
            + sl(w_north) * d[:-2, 1:-1]
            + sl(w_south) * d[2:, 1:-1]
            + sl(w_west) * d[1:-1, :-2]
            + sl(w_east) * d[1:-1, 2:]
        )
        d = jnp.where(sl(mask), summed / sl(denom), 0.0)
    return d


def shift_cols(a, toward):
    zero = jnp.zeros(a.shape[:-1] + (1,), a.dtype)
    if toward == "west":
        return jnp.concatenate([zero, a[..., :-1]], axis=-1)
    return jnp.concatenate([a[..., 1:], zero], axis=-1)


def thermal_sweeps(temp_ext, source_ext, lat_ext, vert_ext, inside):
    lk = lat_ext[1:-1, 1:-1]
    vk = vert_ext[1:-1, 1:-1]
    w_north = (lk + lat_ext[1:-1, :-2]) * 0.5
    w_south = (lk + lat_ext[1:-1, 2:]) * 0.5
    w_west = (lk + shift_cols(lk, "west")) * 0.5
    w_east = (lk + shift_cols(lk, "east")) * 0.5
    w_below = (vk + vert_ext[:-2, 1:-1]) * 0.5
    w_above = (vk + vert_ext[2:, 1:-1]) * 0.5
    denom = w_north + w_south + w_west + w_east + w_below + w_above
    source = source_ext[1:-1, 1:-1]
    mask = inside[1:-1, 1:-1]
    t = temp_ext
    for s in range(HEAT_SWEEPS):
        o = s
        e0 = denom.shape[0] - s
        e1 = denom.shape[1] - s
        sl = lambda a: a[o:e0, o:e1]
        mid = t[1:-1, 1:-1]
        summed = (
            sl(source)
            + sl(w_north) * t[1:-1, :-2]
            + sl(w_south) * t[1:-1, 2:]
            + sl(w_west) * shift_cols(mid, "west")
            + sl(w_east) * shift_cols(mid, "east")
            + sl(w_below) * t[:-2, 1:-1]
            + sl(w_above) * t[2:, 1:-1]
        )
        t = jnp.where(sl(mask), summed / sl(denom), 0.0)
    return t


def body(demand, leakage, conductance, vias, layer_of, lateral_k, vertical_k):
    h = HALO
    tile_rows, tile_cols = demand.shape
    group_layers, cell_rows, therm_cols = lateral_k.shape
    cell_cols = tile_cols // COARSE
    n_r = lax.axis_size("row")
    n_c = lax.axis_size("col")
    r_idx = lax.axis_index("row")
    c_idx = lax.axis_index("col")
    all_layers = group_layers * n_c
    all_rows = cell_rows * n_r

    via_g = VIA_CONDUCT * vias.astype(jnp.float32)
    load0 = demand + leakage

    power_sides = (("row", 1), ("col", 2))
    therm_sides = (("row", 2), ("col", 1))
    p_ext = extended(jnp.stack([conductance, load0, via_g]), power_sides, h)
    cond0_ext, load0_ext, via_ext = p_ext[0], p_ext[1], p_ext[2]
    k_ext = extended(jnp.stack([lateral_k, vertical_k]), therm_sides, h)
    lat_ext, vert_ext = k_ext[0], k_ext[1]
    layer_ext = extended(layer_of, (("row", 0),), h)

    prow = r_idx * tile_rows - h + jnp.arange(tile_rows + 2 * h, dtype=jnp.int32)
    pcol = c_idx * tile_cols - h + jnp.arange(tile_cols + 2 * h, dtype=jnp.int32)
    p_inside = ((prow >= 0) & (prow < tile_rows * n_r))[:, None] & ((pcol >= 0) & (pcol < tile_cols * n_c))[None, :]
    tlay = c_idx * group_layers - h + jnp.arange(group_layers + 2 * h, dtype=jnp.int32)
    trow = r_idx * cell_rows - h + jnp.arange(cell_rows + 2 * h, dtype=jnp.int32)
    t_inside = (((tlay >= 0) & (tlay < all_layers))[:, None] & ((trow >= 0) & (trow < all_rows))[None, :])[:, :, None]
    picker_ext = (layer_ext[None, :, :] == tlay[:, None, None]) & t_inside
    own_layers = c_idx * group_layers + jnp.arange(group_layers, dtype=jnp.int32)
    picker_own = layer_of[None, :, :] == own_layers[:, None, None]

    drop = None
    temp = None
    drop_ext = jnp.zeros(cond0_ext.shape, jnp.float32)
    temp_ext = jnp.zeros(lat_ext.shape, jnp.float32)
    cond_ext = cond0_ext
    load_ext = load0_ext
    for outer in range(OUTER):
        if outer > 0:
            partial = jnp.sum(jnp.where(picker_own, temp, 0.0), axis=0)
            band = lax.psum(partial, "col")
            cell_temp = lax.dynamic_slice_in_dim(band, c_idx * cell_cols, cell_cols, 1)
            denom_c = 1.0 + COND_SLOPE * cell_temp
            grow_c = jnp.exp(LEAK_SLOPE * cell_temp)
            denom_f = fine_of(denom_c, tile_cols)
            grow_f = fine_of(grow_c, tile_cols)
            cond = conductance / denom_f
            load = demand + leakage * grow_f
            p_ext = extended(jnp.stack([drop, cond, load]), power_sides, h)
            drop_ext, cond_ext, load_ext = p_ext[0], p_ext[1], p_ext[2]
            temp_ext = extended(temp, (("row", 1), ("col", 0)), h)
        drop = power_sweeps(drop_ext, cond_ext, load_ext, via_ext, p_inside)
        cond_own = cond_ext[h:-h, h:-h]
        load_own = load_ext[h:-h, h:-h]
        heat = coarse_of(load_own * (1.0 - drop) + cond_own * drop * drop)
        heat_rows = extended(heat, (("row", 0),), h)
        gathered = lax.all_gather(heat_rows, "col", axis=0, tiled=False)
        heat_ext = gathered.transpose(1, 0, 2).reshape(cell_rows + 2 * h, n_c * cell_cols)
        source_ext = jnp.where(picker_ext, heat_ext[None, :, :], 0.0)
        temp = thermal_sweeps(temp_ext, source_ext, lat_ext, vert_ext, t_inside)
    return (drop, temp)


def solution(mesh):
    in_specs = (
        P("row", "col"),
        P("row", "col"),
        P("row", "col"),
        P("row", "col"),
        P("row", None),
        P("col", "row", None),
        P("col", "row", None),
    )
    out_specs = (P("row", "col"), P("col", "row", None))
    return jax.shard_map(body, mesh=mesh, in_specs=in_specs, out_specs=out_specs, check_vma=False)
```

profile of v0, /device:TPU:8, one launch (start us, length us, event | category | flops | bytes accessed | tf_op | source)
XLA Modules:
  0.0 282.0 jit_solution(17460665195513601387)
XLA Ops:
  7.2 2.2 multiply_bitcast_fusion
  9.5 0.9 copy-done.14
  10.8 1.9 collective-permute-start.1
  12.7 2.4 collective-permute-start
  15.1 1.3 fusion.168
  16.5 3.1 %collective-permute-start.5 = (s32[4,512]{1,0:T(4,128)}, s32[4,512]{1,0:T(4,128)}, u32[]{:S(2)}, u32[]{:S(2)}) collective-permute-start(s32[4,512]{1,0:T(4,128)} %get-tuple-element.68), channel_id=1, source_target_pairs={{4,0},{8,4},{12,8},{16,12},{20,16},{24,20},{28,24},{5,1},{9,5},{13... | collective-permute-start | bytes 24584 | tf_op jit(solution)/shard_map/ppermute | solution.py:27
  19.6 1.9 collective-permute-start.4
  21.6 0.7 pad_maximum_fusion.7
  22.3 3.6 %collective-permute-start.9 = (f32[2,8,4,512]{3,2,1,0:T(4,128)}, f32[2,8,4,512]{3,2,1,0:T(4,128)}, u32[]{:S(2)}, u32[]{:S(2)}) collective-permute-start(f32[2,8,4,512]{3,2,1,0:T(4,128)} %get-tuple-element.54), channel_id=1, source_target_pairs={{4,0},{8,4},{12,8},{16,12},{20,16},{24,20},{28,24},{5,1},{9,5},{13... | collective-permute-start | bytes 393224 | tf_op jit(solution)/shard_map/ppermute | solution.py:27
  31.3 2.3 pad_maximum_fusion
  33.7 4.2 %collective-permute-start.2 = (f32[3,264,4]{2,1,0:T(8,128)S(1)}, f32[3,264,4]{2,1,0:T(8,128)}, u32[]{:S(2)}, u32[]{:S(2)}) collective-permute-start(f32[3,264,4]{2,1,0:T(8,128)S(1)} %get-tuple-element.36), channel_id=1, source_target_pairs={{0,1},{1,2},{2,3},{4,5},{5,6},{6,7},{8,9},{9,10},{10,11},{12,13},{... | collective-permute-start | bytes 38024 | tf_op jit(solution)/shard_map/ppermute | solution.py:24
  37.9 1.3 collective-permute-start.3
  39.8 6.1 %collective-permute-done.2 = f32[3,264,4]{2,1,0:T(8,128)} collective-permute-done((f32[3,264,4]{2,1,0:T(8,128)S(1)}, f32[3,264,4]{2,1,0:T(8,128)}, u32[]{:S(2)}, u32[]{:S(2)}) %collective-permute-start.2) | collective-permute-done | bytes 12704 | tf_op jit(solution)/shard_map/ppermute | solution.py:24
  45.9 1.9 collective-permute-start.8
  47.8 8.8 %collective-permute-done.3 = f32[3,264,4]{2,1,0:T(8,128)} collective-permute-done((f32[3,264,4]{2,1,0:T(8,128)S(1)}, f32[3,264,4]{2,1,0:T(8,128)}, u32[]{:S(2)}, u32[]{:S(2)}) %collective-permute-start.3) | collective-permute-done | bytes 12704 | tf_op jit(solution)/shard_map/ppermute | solution.py:27
  56.6 4.6 %concatenate.88 = f32[3,264,1032]{2,1,0:T(8,128)} concatenate(f32[3,264,4]{2,1,0:T(8,128)} %collective-permute-done.2, f32[3,264,1024]{2,1,0:T(8,128)S(1)} %pad_maximum_fusion, f32[3,264,4]{2,1,0:T(8,128)} %collective-permute-done.3), dimensions={2} | concatenate | bytes 6538752 | tf_op jit(solution)/shard_map/concatenate | solution.py:28
  61.2 2.3 slice_bitcast_fusion.5
  63.5 2.4 fusion.36
  65.9 4.5 %fusion.27 = f32[260,1028]{1,0:T(8,128)S(1)} fusion(f32[262,1030]{1,0:T(8,128)S(1)} %get-tuple-element.22, f32[262,1030]{1,0:T(8,128)S(1)} %get-tuple-element.21, f32[262,1030]{1,0:T(8,128)S(1)} %get-tuple-element.26, f32[262,1030]{1,0:T(8,128)S(1)} %get-tuple-element.25, f32[262,1030]{1,0:T(8,128)S(1)} %get-tuple-element.23, ...), kind=kLoop, calls=%fused_computation.64 | loop fusion | flops 2672800 | bytes 12027600 | tf_op jit(solution)/shard_map/jit(_where)/select_n | solution.py:77
  70.4 4.5 %fusion.22 = f32[258,1026]{1,0:T(8,128)S(1)} fusion(f32[262,1030]{1,0:T(8,128)S(1)} %get-tuple-element.22, f32[260,1028]{1,0:T(8,128)S(1)} %fusion.27, f32[262,1030]{1,0:T(8,128)S(1)} %get-tuple-element.26, f32[262,1030]{1,0:T(8,128)S(1)} %get-tuple-element.25, f32[262,1030]{1,0:T(8,128)S(1)} %get-tuple-element.23, f32[262,1030]{1,0:T(8,128)S(1)} %get-tuple-element.24, ...), kind=kLoop, calls=%fused_computation.54 | loop fusion | flops 2647080 | bytes 11911860 | tf_op jit(solution)/shard_map/jit(_where)/select_n | solution.py:77
  74.9 4.8 %fusion.54 = (f32[32,1024]{1,0:T(8,128)S(1)}, f32[256,1024]{1,0:T(8,128)}) fusion(f32[264,1032]{1,0:T(8,128)S(1)} %get-tuple-element.31, f32[264,1032]{1,0:T(8,128)S(1)} %get-tuple-element.32, f32[262,1030]{1,0:T(8,128)S(1)} %get-tuple-element.22, f32[258,1026]{1,0:T(8,128)S(1)} %fusion.22, f32[262,1030]{1,0:T(8,128)S(1)} %get-tuple-element.26, ...), kind=kLoop, calls=%fused_computation.119 | loop fusion | flops 4161536 | bytes 12976128 | tf_op jit(solution)/shard_map/reduce_sum | solution.py:47
  80.1 1.2 pad_maximum_fusion.3
  81.5 1.3 collective-permute-start.11
  82.8 4.6 %collective-permute-start.10 = (f32[2,4,40,512]{3,2,1,0:T(8,128)S(1)}, f32[2,4,40,512]{3,2,1,0:T(8,128)S(1)}, u32[]{:S(2)}, u32[]{:S(2)}) collective-permute-start(f32[2,4,40,512]{3,2,1,0:T(8,128)S(1)} %get-tuple-element.47), channel_id=1, source_target_pairs={{0,1},{1,2},{2,3},{4,5},{5,6},{6,7},{8,9},{9,10},{10,11},{12,13},{... | collective-permute-start | bytes 1966088 | tf_op jit(solution)/shard_map/ppermute | solution.py:24
  87.4 1.9 collective-permute-start.7
  89.3 2.4 collective-permute-start.6
  91.8 0.7 pad_add_fusion.2
  92.5 1.7 collective-permute-done.6
  94.2 20.9 %all-gather = f32[160,128]{1,0:T(8,128)S(1)} all-gather(f32[40,128]{1,0:T(8,128)S(1)} %pad_maximum_fusion.14), channel_id=2, replica_groups=mesh['row'=8,'col'=4] {'col'}, dimensions={0}, use_global_device_ids=true | all-gather | bytes 102400 | tf_op jit(solution)/shard_map/all_gather | solution.py:178
  115.5 1.4 pad_maximum_fusion.2
  117.8 2.1 fusion.51
  120.6 2.4 fusion.81
  123.6 1.7 fusion.97
  126.0 2.5 select_reduce_fusion
  128.5 42.9 %all-reduce.19.cloned.1.call-done = f32[32,512]{1,0:T(8,128)} async-done(((f32[32,512]{1,0:T(8,128)}), f32[32,512]{1,0:T(8,128)}) %all-reduce.19.cloned.1.call-update) | async-done | bytes 65552 | tf_op jit(solution)/shard_map/psum | solution.py:162
  171.5 1.0 fusion.119
  172.5 1.9 fusion.69
  174.4 1.1 fusion.120
  175.7 2.1 collective-permute-start.13
  177.8 2.4 collective-permute-start.12
  180.2 3.2 %collective-permute-start.19 = (f32[8,4,512]{2,1,0:T(4,128)S(1)}, f32[8,4,512]{2,1,0:T(4,128)S(1)}, u32[]{:S(2)}, u32[]{:S(2)}) collective-permute-start(f32[8,4,512]{2,1,0:T(4,128)S(1)} %get-tuple-element.66), channel_id=1, source_target_pairs={{4,0},{8,4},{12,8},{16,12},{20,16},{24,20},{28,24},{5,1},{9,5},{13... | collective-permute-start | bytes 196616 | tf_op jit(solution)/shard_map/ppermute | solution.py:27
  183.4 1.9 collective-permute-start.18
  185.3 0.7 pad_maximum_fusion.1
  186.1 1.7 copy-done.12
  187.9 4.2 %collective-permute-start.14 = (f32[3,264,4]{2,1,0:T(8,128)S(1)}, f32[3,264,4]{2,1,0:T(8,128)}, u32[]{:S(2)}, u32[]{:S(2)}) collective-permute-start(f32[3,264,4]{2,1,0:T(8,128)S(1)} %get-tuple-element.34), channel_id=1, source_target_pairs={{0,1},{1,2},{2,3},{4,5},{5,6},{6,7},{8,9},{9,10},{10,11},{12,13},{... | collective-permute-start | bytes 38024 | tf_op jit(solution)/shard_map/ppermute | solution.py:24
  192.1 1.3 collective-permute-start.15
  193.4 0.9 pad_maximum_fusion.5
  194.3 6.1 %collective-permute-done.14 = f32[3,264,4]{2,1,0:T(8,128)} collective-permute-done((f32[3,264,4]{2,1,0:T(8,128)S(1)}, f32[3,264,4]{2,1,0:T(8,128)}, u32[]{:S(2)}, u32[]{:S(2)}) %collective-permute-start.14) | collective-permute-done | bytes 12704 | tf_op jit(solution)/shard_map/ppermute | solution.py:24
  200.4 10.6 %collective-permute-done.15 = f32[3,264,4]{2,1,0:T(8,128)} collective-permute-done((f32[3,264,4]{2,1,0:T(8,128)S(1)}, f32[3,264,4]{2,1,0:T(8,128)}, u32[]{:S(2)}, u32[]{:S(2)}) %collective-permute-start.15) | collective-permute-done | bytes 12704 | tf_op jit(solution)/shard_map/ppermute | solution.py:27
  211.1 5.2 %concatenate.103 = f32[3,264,1032]{2,1,0:T(8,128)} concatenate(f32[3,264,4]{2,1,0:T(8,128)} %collective-permute-done.14, f32[3,264,1024]{2,1,0:T(8,128)} %copy-done.12, f32[3,264,4]{2,1,0:T(8,128)} %collective-permute-done.15), dimensions={2} | concatenate | bytes 6538752 | tf_op jit(solution)/shard_map/concatenate | solution.py:28
  216.3 2.4 slice_bitcast_fusion.2
  218.7 3.7 %fusion.14 = (f32[262,1030]{1,0:T(8,128)S(1)}, f32[262,1030]{1,0:T(8,128)S(1)}, f32[262,1030]{1,0:T(8,128)S(1)}, f32[262,1030]{1,0:T(8,128)S(1)}, f32[262,1030]{1,0:T(8,128)S(1)}) fusion(f32[264,1032]{1,0:T(8,128)S(1)} %get-tuple-element.27, f32[264,1032]{1,0:T(8,128)S(1)} %get-tuple-element.29, pred[264,1032]{1,0:T(8,128)(4,1)S(1)} %copy-done.9, ...), kind=kLoop, calls=%fused_computation.35 | loop fusion | flops 5936920 | bytes 17540900 | tf_op jit(solution)/shard_map/jit(_where)/select_n | solution.py:77
  223.2 4.5 %fusion.7 = f32[260,1028]{1,0:T(8,128)S(1)} fusion(f32[262,1030]{1,0:T(8,128)S(1)} %add_add_fusion, f32[262,1030]{1,0:T(8,128)S(1)} %get-tuple-element.4, f32[262,1030]{1,0:T(8,128)S(1)} %get-tuple-element.8, f32[262,1030]{1,0:T(8,128)S(1)} %get-tuple-element.7, f32[262,1030]{1,0:T(8,128)S(1)} %get-tuple-element.5, f32[262,1030]{1,0:T(8,128)S(1)} %get-tuple-element.6, ...), kind=kLoop, calls=%fused_computation.23 | loop fusion | flops 2672800 | bytes 12027600 | tf_op jit(solution)/shard_map/jit(_where)/select_n | solution.py:77
  227.7 4.7 %fusion.2 = f32[258,1026]{1,0:T(8,128)S(1)} fusion(f32[262,1030]{1,0:T(8,128)S(1)} %add_add_fusion, f32[260,1028]{1,0:T(8,128)S(1)} %fusion.7, f32[262,1030]{1,0:T(8,128)S(1)} %get-tuple-element.8, f32[262,1030]{1,0:T(8,128)S(1)} %get-tuple-element.7, f32[262,1030]{1,0:T(8,128)S(1)} %get-tuple-element.5, f32[262,1030]{1,0:T(8,128)S(1)} %get-tuple-element.6, ...), kind=kLoop, calls=%fused_computation.13 | loop fusion | flops 2647080 | bytes 11911860 | tf_op jit(solution)/shard_map/jit(_where)/select_n | solution.py:77
  232.3 4.4 %fusion.57 = (f32[32,1024]{1,0:T(8,128)S(1)}, f32[256,1024]{1,0:T(8,128)}) fusion(f32[264,1032]{1,0:T(8,128)S(1)} %get-tuple-element.28, f32[264,1032]{1,0:T(8,128)S(1)} %get-tuple-element.29, f32[262,1030]{1,0:T(8,128)S(1)} %add_add_fusion, f32[258,1026]{1,0:T(8,128)S(1)} %fusion.2, f32[262,1030]{1,0:T(8,128)S(1)} %get-tuple-element.8, ...), kind=kLoop, calls=%fused_computation.122 | loop fusion | flops 4161536 | bytes 12976128 | tf_op jit(solution)/shard_map/reduce_sum | solution.py:47
  237.2 2.3 collective-permute-start.17
  239.5 2.0 collective-permute-start.16
  241.6 1.4 collective-permute-start.21
  243.1 4.6 %collective-permute-start.20 = (f32[4,40,512]{2,1,0:T(8,128)S(1)}, f32[4,40,512]{2,1,0:T(8,128)S(1)}, u32[]{:S(2)}, u32[]{:S(2)}) collective-permute-start(f32[4,40,512]{2,1,0:T(8,128)S(1)} %get-tuple-element.63), channel_id=1, source_target_pairs={{0,1},{1,2},{2,3},{4,5},{5,6},{6,7},{8,9},{9,10},{10,11},{12,13},{... | collective-permute-start | bytes 983048 | tf_op jit(solution)/shard_map/ppermute | solution.py:24
  247.7 14.6 %all-gather.1 = f32[160,128]{1,0:T(8,128)S(1)} all-gather(f32[40,128]{1,0:T(8,128)S(1)} %pad_maximum_fusion.15), channel_id=3, replica_groups=mesh['row'=8,'col'=4] {'col'}, dimensions={0}, use_global_device_ids=true | all-gather | bytes 102400 | tf_op jit(solution)/shard_map/all_gather | solution.py:178
  265.2 2.0 fusion.39
  267.8 2.4 fusion.73
  270.6 1.8 fusion.89
  273.1 1.9 fusion.105
  (148 shorter events, 16.4 us)
Async XLA Ops:
  7.2 2.3 copy-start.16
  7.2 164.3 %all-reduce.19.cloned.1.call-start = ((), (), s32[]{:S(2)}) async-start(), calls=%async_computation | async-start | bytes 131072 | tf_op jit(solution)/shard_map/psum | solution.py:162
  9.5 1.0 copy-start.14
  9.5 1.3 copy-start.15
  9.5 12.1 %copy-start.20 = (f32[8,32,512]{2,1,0:T(8,128)S(1)}, f32[8,32,512]{2,1,0:T(8,128)}, u32[]{:S(2)}) copy-start(f32[8,32,512]{2,1,0:T(8,128)} %param.13) | copy-start | bytes 1572868
  9.5 12.1 %copy-start.22 = (f32[8,32,512]{2,1,0:T(8,128)S(1)}, f32[8,32,512]{2,1,0:T(8,128)}, u32[]{:S(2)}) copy-start(f32[8,32,512]{2,1,0:T(8,128)} %param.12) | copy-start | bytes 1572868
  10.8 19.9 %collective-permute-start.1 = (f32[3,4,1024]{2,1,0:T(4,128)S(1)}, f32[3,4,1024]{2,1,0:T(4,128)S(1)}, u32[]{:S(2)}, u32[]{:S(2)}) collective-permute-start(f32[3,4,1024]{2,1,0:T(4,128)S(1)} %get-tuple-element.40), channel_id=1, source_target_pairs={{4,0},{8,4},{12,8},{16,12},{20,16},{24,20},{28,24},{5,1},{9,5},{13... | collective-permute-start | bytes 147464 | tf_op jit(solution)/shard_map/ppermute | solution.py:27
  12.7 18.6 %collective-permute-start = (f32[3,4,1024]{2,1,0:T(4,128)S(1)}, f32[3,4,1024]{2,1,0:T(4,128)}, u32[]{:S(2)}, u32[]{:S(2)}) collective-permute-start(f32[3,4,1024]{2,1,0:T(4,128)S(1)} %get-tuple-element.39), channel_id=1, source_target_pairs={{0,4},{4,8},{8,12},{12,16},{16,20},{20,24},{24,28},{1,5},{5,9},{9,... | collective-permute-start | bytes 147464 | tf_op jit(solution)/shard_map/ppermute | solution.py:24
  16.5 72.9 %collective-permute-start.5 = (s32[4,512]{1,0:T(4,128)}, s32[4,512]{1,0:T(4,128)}, u32[]{:S(2)}, u32[]{:S(2)}) collective-permute-start(s32[4,512]{1,0:T(4,128)} %get-tuple-element.68), channel_id=1, source_target_pairs={{4,0},{8,4},{12,8},{16,12},{20,16},{24,20},{28,24},{5,1},{9,5},{13... | collective-permute-start | bytes 24584 | tf_op jit(solution)/shard_map/ppermute | solution.py:27
  19.6 72.1 %collective-permute-start.4 = (s32[4,512]{1,0:T(4,128)}, s32[4,512]{1,0:T(4,128)}, u32[]{:S(2)}, u32[]{:S(2)}) collective-permute-start(s32[4,512]{1,0:T(4,128)} %get-tuple-element.67), channel_id=1, source_target_pairs={{0,4},{4,8},{8,12},{12,16},{16,20},{20,24},{24,28},{1,5},{5,9},{9,... | collective-permute-start | bytes 24584 | tf_op jit(solution)/shard_map/ppermute | solution.py:24
  22.3 57.8 %collective-permute-start.9 = (f32[2,8,4,512]{3,2,1,0:T(4,128)}, f32[2,8,4,512]{3,2,1,0:T(4,128)}, u32[]{:S(2)}, u32[]{:S(2)}) collective-permute-start(f32[2,8,4,512]{3,2,1,0:T(4,128)} %get-tuple-element.54), channel_id=1, source_target_pairs={{4,0},{8,4},{12,8},{16,12},{20,16},{24,20},{28,24},{5,1},{9,5},{13... | collective-permute-start | bytes 393224 | tf_op jit(solution)/shard_map/ppermute | solution.py:27
  30.1 44.8 %copy-start.8 = (pred[264,1032]{1,0:T(8,128)(4,1)}, pred[264,1032]{1,0:T(8,128)(4,1)S(1)}, u32[]{:S(2)}) copy-start(pred[264,1032]{1,0:T(8,128)(4,1)S(1)} %broadcast_and_fusion) | copy-start | bytes 817348
  33.7 12.1 %collective-permute-start.2 = (f32[3,264,4]{2,1,0:T(8,128)S(1)}, f32[3,264,4]{2,1,0:T(8,128)}, u32[]{:S(2)}, u32[]{:S(2)}) collective-permute-start(f32[3,264,4]{2,1,0:T(8,128)S(1)} %get-tuple-element.36), channel_id=1, source_target_pairs={{0,1},{1,2},{2,3},{4,5},{5,6},{6,7},{8,9},{9,10},{10,11},{12,13},{... | collective-permute-start | bytes 38024 | tf_op jit(solution)/shard_map/ppermute | solution.py:24
  37.9 18.7 %collective-permute-start.3 = (f32[3,264,4]{2,1,0:T(8,128)S(1)}, f32[3,264,4]{2,1,0:T(8,128)}, u32[]{:S(2)}, u32[]{:S(2)}) collective-permute-start(f32[3,264,4]{2,1,0:T(8,128)S(1)} %get-tuple-element.35), channel_id=1, source_target_pairs={{1,0},{2,1},{3,2},{5,4},{6,5},{7,6},{9,8},{10,9},{11,10},{13,12},{... | collective-permute-start | bytes 38024 | tf_op jit(solution)/shard_map/ppermute | solution.py:27
  45.9 34.2 %collective-permute-start.8 = (f32[2,8,4,512]{3,2,1,0:T(4,128)}, f32[2,8,4,512]{3,2,1,0:T(4,128)}, u32[]{:S(2)}, u32[]{:S(2)}) collective-permute-start(f32[2,8,4,512]{3,2,1,0:T(4,128)} %get-tuple-element.53), channel_id=1, source_target_pairs={{0,4},{4,8},{8,12},{12,16},{16,20},{20,24},{24,28},{1,5},{5,9},{9,... | collective-permute-start | bytes 393224 | tf_op jit(solution)/shard_map/ppermute | solution.py:24
  63.5 2.4 copy-start.10
  74.9 5.2 %copy-start.21 = (f32[8,32,512]{2,1,0:T(8,128)S(1)}, f32[8,32,512]{2,1,0:T(8,128)}, u32[]{:S(2)}) copy-start(f32[8,32,512]{2,1,0:T(8,128)} %param.13) | copy-start | bytes 1572868
  74.9 5.2 %copy-start.23 = (f32[8,32,512]{2,1,0:T(8,128)S(1)}, f32[8,32,512]{2,1,0:T(8,128)}, u32[]{:S(2)}) copy-start(f32[8,32,512]{2,1,0:T(8,128)} %param.12) | copy-start | bytes 1572868
  81.3 10.4 %copy-start.25 = (s32[32,512]{1,0:T(8,128)S(1)}, s32[32,512]{1,0:T(8,128)}, u32[]{:S(2)}) copy-start(s32[32,512]{1,0:T(8,128)} %param.11) | copy-start | bytes 196612
  81.3 33.9 %copy-start.32 = (pred[16,40]{1,0:T(8,128)(4,1)S(1)}, pred[16,40]{1,0:T(8,128)(4,1)}, u32[]{:S(2)}) copy-start(pred[16,40]{1,0:T(8,128)(4,1)} %broadcast_and_fusion.1) | copy-start | bytes 1924
  81.3 33.9 %copy-start.39 = (s32[16]{0:T(128)S(1)}, s32[16]{0:T(128)}, u32[]{:S(2)}) copy-start(s32[16]{0:T(128)} %iota_add_fusion.2) | copy-start | bytes 196
  81.5 34.0 %collective-permute-start.11 = (f32[2,4,40,512]{3,2,1,0:T(8,128)S(1)}, f32[2,4,40,512]{3,2,1,0:T(8,128)S(1)}, u32[]{:S(2)}, u32[]{:S(2)}) collective-permute-start(f32[2,4,40,512]{3,2,1,0:T(8,128)S(1)} %get-tuple-element.48), channel_id=1, source_target_pairs={{1,0},{2,1},{3,2},{5,4},{6,5},{7,6},{9,8},{10,9},{11,10},{13,12},{... | collective-permute-start | bytes 1966088 | tf_op jit(solution)/shard_map/ppermute | solution.py:27
  82.8 32.7 %collective-permute-start.10 = (f32[2,4,40,512]{3,2,1,0:T(8,128)S(1)}, f32[2,4,40,512]{3,2,1,0:T(8,128)S(1)}, u32[]{:S(2)}, u32[]{:S(2)}) collective-permute-start(f32[2,4,40,512]{3,2,1,0:T(8,128)S(1)} %get-tuple-element.47), channel_id=1, source_target_pairs={{0,1},{1,2},{2,3},{4,5},{5,6},{6,7},{8,9},{9,10},{10,11},{12,13},{... | collective-permute-start | bytes 1966088 | tf_op jit(solution)/shard_map/ppermute | solution.py:24
  87.4 5.1 %collective-permute-start.7 = (f32[4,128]{1,0:T(4,128)S(1)}, f32[4,128]{1,0:T(4,128)S(1)}, u32[]{:S(2)}, u32[]{:S(2)}) collective-permute-start(f32[4,128]{1,0:T(4,128)S(1)} %get-tuple-element.72), channel_id=1, source_target_pairs={{4,0},{8,4},{12,8},{16,12},{20,16},{24,20},{28,24},{5,1},{9,5},{13... | collective-permute-start | bytes 6152 | tf_op jit(solution)/shard_map/ppermute | solution.py:27
  89.3 4.9 %collective-permute-start.6 = (f32[4,128]{1,0:T(4,128)S(1)}, f32[4,128]{1,0:T(4,128)S(1)}, u32[]{:S(2)}, u32[]{:S(2)}) collective-permute-start(f32[4,128]{1,0:T(4,128)S(1)} %get-tuple-element.71), channel_id=1, source_target_pairs={{0,4},{4,8},{8,12},{12,16},{16,20},{20,24},{24,28},{1,5},{5,9},{9,... | collective-permute-start | bytes 6152 | tf_op jit(solution)/shard_map/ppermute | solution.py:24
  117.2 0.7 copy-start.33
  117.2 0.6 copy-start.38
  119.9 5.7 %copy-start = (f32[14,38,512]{2,1,0:T(8,128)}, f32[14,38,512]{2,1,0:T(8,128)S(1)}, u32[]{:S(2)}) copy-start(f32[14,38,512]{2,1,0:T(8,128)S(1)} %get-tuple-element.15) | copy-start | bytes 3268612
  119.9 5.7 %copy-start.2 = (f32[14,38,512]{2,1,0:T(8,128)}, f32[14,38,512]{2,1,0:T(8,128)S(1)}, u32[]{:S(2)}) copy-start(f32[14,38,512]{2,1,0:T(8,128)S(1)} %get-tuple-element.16) | copy-start | bytes 3268612
  119.9 5.7 %copy-start.4 = (f32[14,38,512]{2,1,0:T(8,128)}, f32[14,38,512]{2,1,0:T(8,128)S(1)}, u32[]{:S(2)}) copy-start(f32[14,38,512]{2,1,0:T(8,128)S(1)} %get-tuple-element.17) | copy-start | bytes 3268612
  120.0 5.7 %copy-start.6 = (f32[14,38,512]{2,1,0:T(8,128)}, f32[14,38,512]{2,1,0:T(8,128)S(1)}, u32[]{:S(2)}) copy-start(f32[14,38,512]{2,1,0:T(8,128)S(1)} %get-tuple-element.18) | copy-start | bytes 3268612
  120.0 0.7 copy-start.34
  123.0 0.6 copy-start.31
  125.3 0.7 copy-start.36
  125.4 0.7 copy-start.41
  172.5 3.0 %copy-start.17 = (f32[256,1024]{1,0:T(8,128)S(1)}, f32[256,1024]{1,0:T(8,128)}, u32[]{:S(2)}) copy-start(f32[256,1024]{1,0:T(8,128)} %param.9) | copy-start | bytes 3145732
  174.3 1.3 copy-start.13
  175.7 4.5 %copy-start.18 = (f32[8,32,512]{2,1,0:T(8,128)S(1)}, f32[8,32,512]{2,1,0:T(8,128)}, u32[]{:S(2)}) copy-start(f32[8,32,512]{2,1,0:T(8,128)} %get-tuple-element.10) | copy-start | bytes 1572868
  175.7 9.6 %collective-permute-start.13 = (f32[3,4,1024]{2,1,0:T(4,128)S(1)}, f32[3,4,1024]{2,1,0:T(4,128)S(1)}, u32[]{:S(2)}, u32[]{:S(2)}) collective-permute-start(f32[3,4,1024]{2,1,0:T(4,128)S(1)} %get-tuple-element.38), channel_id=1, source_target_pairs={{4,0},{8,4},{12,8},{16,12},{20,16},{24,20},{28,24},{5,1},{9,5},{13... | collective-permute-start | bytes 147464 | tf_op jit(solution)/shard_map/ppermute | solution.py:27
  177.8 7.6 %collective-permute-start.12 = (f32[3,4,1024]{2,1,0:T(4,128)S(1)}, f32[3,4,1024]{2,1,0:T(4,128)S(1)}, u32[]{:S(2)}, u32[]{:S(2)}) collective-permute-start(f32[3,4,1024]{2,1,0:T(4,128)S(1)} %get-tuple-element.37), channel_id=1, source_target_pairs={{0,4},{4,8},{8,12},{12,16},{16,20},{20,24},{24,28},{1,5},{5,9},{9,... | collective-permute-start | bytes 147464 | tf_op jit(solution)/shard_map/ppermute | solution.py:24
  180.2 13.1 %collective-permute-start.19 = (f32[8,4,512]{2,1,0:T(4,128)S(1)}, f32[8,4,512]{2,1,0:T(4,128)S(1)}, u32[]{:S(2)}, u32[]{:S(2)}) collective-permute-start(f32[8,4,512]{2,1,0:T(4,128)S(1)} %get-tuple-element.66), channel_id=1, source_target_pairs={{4,0},{8,4},{12,8},{16,12},{20,16},{24,20},{28,24},{5,1},{9,5},{13... | collective-permute-start | bytes 196616 | tf_op jit(solution)/shard_map/ppermute | solution.py:27
  183.4 10.0 %collective-permute-start.18 = (f32[8,4,512]{2,1,0:T(4,128)S(1)}, f32[8,4,512]{2,1,0:T(4,128)S(1)}, u32[]{:S(2)}, u32[]{:S(2)}) collective-permute-start(f32[8,4,512]{2,1,0:T(4,128)S(1)} %get-tuple-element.65), channel_id=1, source_target_pairs={{0,4},{4,8},{8,12},{12,16},{16,20},{20,24},{24,28},{1,5},{5,9},{9,... | collective-permute-start | bytes 196616 | tf_op jit(solution)/shard_map/ppermute | solution.py:24
  186.1 1.7 copy-start.12
  187.9 12.5 %collective-permute-start.14 = (f32[3,264,4]{2,1,0:T(8,128)S(1)}, f32[3,264,4]{2,1,0:T(8,128)}, u32[]{:S(2)}, u32[]{:S(2)}) collective-permute-start(f32[3,264,4]{2,1,0:T(8,128)S(1)} %get-tuple-element.34), channel_id=1, source_target_pairs={{0,1},{1,2},{2,3},{4,5},{5,6},{6,7},{8,9},{9,10},{10,11},{12,13},{... | collective-permute-start | bytes 38024 | tf_op jit(solution)/shard_map/ppermute | solution.py:24
  192.1 19.0 %collective-permute-start.15 = (f32[3,264,4]{2,1,0:T(8,128)S(1)}, f32[3,264,4]{2,1,0:T(8,128)}, u32[]{:S(2)}, u32[]{:S(2)}) collective-permute-start(f32[3,264,4]{2,1,0:T(8,128)S(1)} %get-tuple-element.33), channel_id=1, source_target_pairs={{1,0},{2,1},{3,2},{5,4},{6,5},{7,6},{9,8},{10,9},{11,10},{13,12},{... | collective-permute-start | bytes 38024 | tf_op jit(solution)/shard_map/ppermute | solution.py:27
  193.4 7.1 %copy-start.26 = (f32[8,4,512]{2,1,0:T(4,128)}, f32[8,4,512]{2,1,0:T(4,128)S(1)}, u32[]{:S(2)}) copy-start(f32[8,4,512]{2,1,0:T(4,128)S(1)} %collective-permute-done.19) | copy-start | bytes 196612
  193.4 7.0 %copy-start.28 = (f32[8,4,512]{2,1,0:T(4,128)}, f32[8,4,512]{2,1,0:T(4,128)S(1)}, u32[]{:S(2)}) copy-start(f32[8,4,512]{2,1,0:T(4,128)S(1)} %collective-permute-done.18) | copy-start | bytes 196612
  216.2 2.4 copy-start.9
  216.3 2.5 copy-start.11
  232.3 9.2 %copy-start.24 = (f32[8,40,512]{2,1,0:T(8,128)S(1)}, f32[8,40,512]{2,1,0:T(8,128)}, u32[]{:S(2)}) copy-start(f32[8,40,512]{2,1,0:T(8,128)} %pad_maximum_fusion.5) | copy-start | bytes 1966084
  236.8 25.6 %copy-start.40 = (s32[16]{0:T(128)S(1)}, s32[16]{0:T(128)}, u32[]{:S(2)}) copy-start(s32[16]{0:T(128)} %iota_add_fusion.2) | copy-start | bytes 196
  237.2 10.4 %collective-permute-start.17 = (f32[4,128]{1,0:T(4,128)S(1)}, f32[4,128]{1,0:T(4,128)S(1)}, u32[]{:S(2)}, u32[]{:S(2)}) collective-permute-start(f32[4,128]{1,0:T(4,128)S(1)} %get-tuple-element.70), channel_id=1, source_target_pairs={{4,0},{8,4},{12,8},{16,12},{20,16},{24,20},{28,24},{5,1},{9,5},{13... | collective-permute-start | bytes 6152 | tf_op jit(solution)/shard_map/ppermute | solution.py:27
  239.5 8.1 %collective-permute-start.16 = (f32[4,128]{1,0:T(4,128)S(1)}, f32[4,128]{1,0:T(4,128)S(1)}, u32[]{:S(2)}, u32[]{:S(2)}) collective-permute-start(f32[4,128]{1,0:T(4,128)S(1)} %get-tuple-element.69), channel_id=1, source_target_pairs={{0,4},{4,8},{8,12},{12,16},{16,20},{20,24},{24,28},{1,5},{5,9},{9,... | collective-permute-start | bytes 6152 | tf_op jit(solution)/shard_map/ppermute | solution.py:24
  241.6 21.1 %copy-start.19 = (f32[8,32,512]{2,1,0:T(8,128)S(1)}, f32[8,32,512]{2,1,0:T(8,128)}, u32[]{:S(2)}) copy-start(f32[8,32,512]{2,1,0:T(8,128)} %get-tuple-element.10) | copy-start | bytes 1572868
  241.6 21.1 %copy-start.27 = (f32[8,4,512]{2,1,0:T(4,128)S(1)}, f32[8,4,512]{2,1,0:T(4,128)}, u32[]{:S(2)}) copy-start(f32[8,4,512]{2,1,0:T(4,128)} %copy-done.26) | copy-start | bytes 196612
  241.6 21.1 %copy-start.29 = (f32[8,4,512]{2,1,0:T(4,128)S(1)}, f32[8,4,512]{2,1,0:T(4,128)}, u32[]{:S(2)}) copy-start(f32[8,4,512]{2,1,0:T(4,128)} %copy-done.28) | copy-start | bytes 196612
  241.6 21.0 %collective-permute-start.21 = (f32[4,40,512]{2,1,0:T(8,128)S(1)}, f32[4,40,512]{2,1,0:T(8,128)S(1)}, u32[]{:S(2)}, u32[]{:S(2)}) collective-permute-start(f32[4,40,512]{2,1,0:T(8,128)S(1)} %get-tuple-element.64), channel_id=1, source_target_pairs={{1,0},{2,1},{3,2},{5,4},{6,5},{7,6},{9,8},{10,9},{11,10},{13,12},{... | collective-permute-start | bytes 983048 | tf_op jit(solution)/shard_map/ppermute | solution.py:27
  243.1 19.6 %collective-permute-start.20 = (f32[4,40,512]{2,1,0:T(8,128)S(1)}, f32[4,40,512]{2,1,0:T(8,128)S(1)}, u32[]{:S(2)}, u32[]{:S(2)}) collective-permute-start(f32[4,40,512]{2,1,0:T(8,128)S(1)} %get-tuple-element.63), channel_id=1, source_target_pairs={{0,1},{1,2},{2,3},{4,5},{5,6},{6,7},{8,9},{9,10},{10,11},{12,13},{... | collective-permute-start | bytes 983048 | tf_op jit(solution)/shard_map/ppermute | solution.py:24
  262.9 1.3 copy-start.1
  262.9 1.6 copy-start.3
  262.9 1.9 copy-start.5
  262.9 2.3 copy-start.7
  267.2 0.7 copy-start.35
  272.4 0.7 copy-start.37
  (1 other events, 0.6 us)
Sparse Core Ops, SparseCore 0:
  128.7 42.7 all-reduce.18
where the time goes:
time: 287 us; the launch traced here: 282 us
  waiting for transfers between devices  76.4 us (27%)
  other arithmetic  66.5 us (23%)
  starting transfers between devices  55.9 us (19%)
  blocking collectives  35.5 us (12%)
  local copies, waits for them, and re-layouts  29.4 us (10%)
  between operations  15.5 us (5%)
  matrix products  2.87 us (1%)
    psum x1, waiting for transfers between devices, body(): band = lax.psum(partial, 'col')  42.9 us
    all_gather x2, blocking collectives, body(): gathered = lax.all_gather(heat_rows, 'col', axis=0, tiled=False)  35.5 us
    ppermute x11, starting transfers between devices, extended(): lax.ppermute(lax.slice_in_dim(block, block.shape[dim] - width, None, axis...  32.4 us
    select_n x6, other arithmetic, power_sweeps(): d = jnp.where(sl(mask), summed / sl(denom), 0.0)  24.3 us
    ppermute x11, starting transfers between devices, extended(): lax.ppermute(lax.slice_in_dim(block, 0, width, axis=dim), axis, backward)  23.4 us
    ppermute x11, waiting for transfers between devices, extended(): lax.ppermute(lax.slice_in_dim(block, 0, width, axis=dim), axis, backward)  19.5 us
    select_n x7, other arithmetic, thermal_sweeps(): t = jnp.where(sl(mask), summed / sl(denom), 0.0)  14.1 us
    ppermute x11, waiting for transfers between devices, extended(): lax.ppermute(lax.slice_in_dim(block, block.shape[dim] - width, None, axis...  14 us
  transfers between devices with their start and end apart: 23, of which 6 were waited for; matrix products, arithmetic and copies ran while one was open for 13% of the time, Pallas kernels for 0%

commit v1 on v0

--- a/solution.py
+++ b/solution.py
@@ -159,8 +159,9 @@
     for outer in range(OUTER):
         if outer > 0:
             partial = jnp.sum(jnp.where(picker_own, temp, 0.0), axis=0)
-            band = lax.psum(partial, "col")
-            cell_temp = lax.dynamic_slice_in_dim(band, c_idx * cell_cols, cell_cols, 1)
+            parts = partial.reshape(cell_rows, n_c, cell_cols).transpose(1, 0, 2)
+            parts = lax.all_to_all(parts, "col", split_axis=0, concat_axis=0, tiled=True)
+            cell_temp = jnp.sum(parts, axis=0)
             denom_c = 1.0 + COND_SLOPE * cell_temp
             grow_c = jnp.exp(LEAK_SLOPE * cell_temp)
             denom_f = fine_of(denom_c, tile_cols)
@@ -175,7 +176,8 @@
         load_own = load_ext[h:-h, h:-h]
         heat = coarse_of(load_own * (1.0 - drop) + cond_own * drop * drop)
         heat_rows = extended(heat, (("row", 0),), h)
-        gathered = lax.all_gather(heat_rows, "col", axis=0, tiled=False)
+        copies = jnp.broadcast_to(heat_rows[None], (n_c,) + heat_rows.shape)
+        gathered = lax.all_to_all(copies, "col", split_axis=0, concat_axis=0, tiled=True)
         heat_ext = gathered.transpose(1, 0, 2).reshape(cell_rows + 2 * h, n_c * cell_cols)
         source_ext = jnp.where(picker_ext, heat_ext[None, :, :], 0.0)
         temp = thermal_sweeps(temp_ext, source_ext, lat_ext, vert_ext, t_inside)

time: 287 us -> 249 us (0.87)
  the two profiles are of different devices: /device:TPU:8 before, /device:TPU:14 now
where the time goes in v1:
time: 249 us; the launch traced here: 245 us
  starting transfers between devices  80.4 us (32%)
  other arithmetic  69.6 us (28%)
  waiting for transfers between devices  46.5 us (19%)
  local copies, waits for them, and re-layouts  38.6 us (16%)
  blocking collectives  7.01 us (3%)
    ppermute x11, starting transfers between devices, extended(): lax.ppermute(lax.slice_in_dim(block, 0, width, axis=dim), axis, backward)  37.8 us
    select_n x6, other arithmetic, power_sweeps(): d = jnp.where(sl(mask), summed / sl(denom), 0.0)  24.3 us
    all_to_all x2, starting transfers between devices, body(): lax.all_to_all(copies, 'col', split_axis=0, concat_axis=0, tiled=True)  22.1 us
    all_to_all x2, waiting for transfers between devices, body(): lax.all_to_all(copies, 'col', split_axis=0, concat_axis=0, tiled=True)  21.9 us
    ppermute x11, waiting for transfers between devices, extended(): lax.ppermute(lax.slice_in_dim(block, block.shape[dim] - width, None, axis...  21.3 us
    ppermute x11, starting transfers between devices, extended(): lax.ppermute(lax.slice_in_dim(block, block.shape[dim] - width, None, axis...  20.5 us
    select_n x7, other arithmetic, thermal_sweeps(): t = jnp.where(sl(mask), summed / sl(denom), 0.0)  14.1 us
    concatenate x2, local copies, waits for them, and re-layouts, extended(): block = jnp.concatenate([low, block, high], axis=dim)  9.83 us
  transfers between devices with their start and end apart: 24, of which 7 were waited for; matrix products, arithmetic and copies ran while one was open for 28% of the time, Pallas kernels for 0%

profile of v1, /device:TPU:14, one launch (start us, length us, event | category | flops | bytes accessed | tf_op | source)
XLA Modules:
  0.0 245.3 jit_solution(6523992225300942946)
XLA Ops:
  0.6 2.2 multiply_bitcast_fusion
  4.2 1.9 collective-permute-start.1
  6.2 2.4 collective-permute-start
  8.6 1.4 fusion.164
  9.9 3.1 %collective-permute-start.5 = (s32[4,512]{1,0:T(4,128)}, s32[4,512]{1,0:T(4,128)}, u32[]{:S(2)}, u32[]{:S(2)}) collective-permute-start(s32[4,512]{1,0:T(4,128)} %get-tuple-element.68), channel_id=1, source_target_pairs={{4,0},{8,4},{12,8},{16,12},{20,16},{24,20},{28,24},{5,1},{9,5},{13... | collective-permute-start | bytes 24584 | tf_op jit(solution)/shard_map/ppermute | solution.py:27
  13.1 1.9 collective-permute-start.4
  15.8 3.6 %collective-permute-start.9 = (f32[2,8,4,512]{3,2,1,0:T(4,128)}, f32[2,8,4,512]{3,2,1,0:T(4,128)}, u32[]{:S(2)}, u32[]{:S(2)}) collective-permute-start(f32[2,8,4,512]{3,2,1,0:T(4,128)} %get-tuple-element.54), channel_id=1, source_target_pairs={{4,0},{8,4},{12,8},{16,12},{20,16},{24,20},{28,24},{5,1},{9,5},{13... | collective-permute-start | bytes 393224 | tf_op jit(solution)/shard_map/ppermute | solution.py:27
  24.7 2.3 pad_maximum_fusion
  27.2 1.3 collective-permute-start.2
  28.5 5.3 %collective-permute-start.3 = (f32[3,264,4]{2,1,0:T(8,128)S(1)}, f32[3,264,4]{2,1,0:T(8,128)}, u32[]{:S(2)}, u32[]{:S(2)}) collective-permute-start(f32[3,264,4]{2,1,0:T(8,128)S(1)} %get-tuple-element.35), channel_id=1, source_target_pairs={{1,0},{2,1},{3,2},{5,4},{6,5},{7,6},{9,8},{10,9},{11,10},{13,12},{... | collective-permute-start | bytes 38024 | tf_op jit(solution)/shard_map/ppermute | solution.py:27
  34.4 7.1 %collective-permute-done.2 = f32[3,264,4]{2,1,0:T(8,128)} collective-permute-done((f32[3,264,4]{2,1,0:T(8,128)S(1)}, f32[3,264,4]{2,1,0:T(8,128)}, u32[]{:S(2)}, u32[]{:S(2)}) %collective-permute-start.2) | collective-permute-done | bytes 12704 | tf_op jit(solution)/shard_map/ppermute | solution.py:24
  41.5 1.9 collective-permute-start.8
  43.4 4.7 %concatenate.88 = f32[3,264,1032]{2,1,0:T(8,128)} concatenate(f32[3,264,4]{2,1,0:T(8,128)} %collective-permute-done.2, f32[3,264,1024]{2,1,0:T(8,128)S(1)} %pad_maximum_fusion, f32[3,264,4]{2,1,0:T(8,128)} %collective-permute-done.3), dimensions={2} | concatenate | bytes 6538752 | tf_op jit(solution)/shard_map/concatenate | solution.py:28
  48.0 2.3 slice_bitcast_fusion.5
  50.3 2.4 fusion.36
  52.7 4.5 %fusion.27 = f32[260,1028]{1,0:T(8,128)S(1)} fusion(f32[262,1030]{1,0:T(8,128)S(1)} %get-tuple-element.22, f32[262,1030]{1,0:T(8,128)S(1)} %get-tuple-element.21, f32[262,1030]{1,0:T(8,128)S(1)} %get-tuple-element.26, f32[262,1030]{1,0:T(8,128)S(1)} %get-tuple-element.25, f32[262,1030]{1,0:T(8,128)S(1)} %get-tuple-element.23, ...), kind=kLoop, calls=%fused_computation.64 | loop fusion | flops 2672800 | bytes 12027600 | tf_op jit(solution)/shard_map/jit(_where)/select_n | solution.py:77
  57.2 4.5 %fusion.22 = f32[258,1026]{1,0:T(8,128)S(1)} fusion(f32[262,1030]{1,0:T(8,128)S(1)} %get-tuple-element.22, f32[260,1028]{1,0:T(8,128)S(1)} %fusion.27, f32[262,1030]{1,0:T(8,128)S(1)} %get-tuple-element.26, f32[262,1030]{1,0:T(8,128)S(1)} %get-tuple-element.25, f32[262,1030]{1,0:T(8,128)S(1)} %get-tuple-element.23, f32[262,1030]{1,0:T(8,128)S(1)} %get-tuple-element.24, ...), kind=kLoop, calls=%fused_computation.54 | loop fusion | flops 2647080 | bytes 11911860 | tf_op jit(solution)/shard_map/jit(_where)/select_n | solution.py:77
  61.7 4.8 %fusion.54 = (f32[32,1024]{1,0:T(8,128)S(1)}, f32[256,1024]{1,0:T(8,128)}) fusion(f32[264,1032]{1,0:T(8,128)S(1)} %get-tuple-element.31, f32[264,1032]{1,0:T(8,128)S(1)} %get-tuple-element.32, f32[262,1030]{1,0:T(8,128)S(1)} %get-tuple-element.22, f32[258,1026]{1,0:T(8,128)S(1)} %fusion.22, f32[262,1030]{1,0:T(8,128)S(1)} %get-tuple-element.26, ...), kind=kLoop, calls=%fused_computation.119 | loop fusion | flops 4161536 | bytes 12976128 | tf_op jit(solution)/shard_map/reduce_sum | solution.py:47
  66.9 3.6 %collective-permute-start.7 = (f32[4,128]{1,0:T(4,128)S(1)}, f32[4,128]{1,0:T(4,128)S(1)}, u32[]{:S(2)}, u32[]{:S(2)}) collective-permute-start(f32[4,128]{1,0:T(4,128)S(1)} %get-tuple-element.72), channel_id=1, source_target_pairs={{4,0},{8,4},{12,8},{16,12},{20,16},{24,20},{28,24},{5,1},{9,5},{13... | collective-permute-start | bytes 6152 | tf_op jit(solution)/shard_map/ppermute | solution.py:27
  70.6 1.9 collective-permute-start.6
  72.5 1.2 pad_maximum_fusion.3
  73.9 5.9 %collective-permute-start.11 = (f32[2,4,40,512]{3,2,1,0:T(8,128)S(1)}, f32[2,4,40,512]{3,2,1,0:T(8,128)S(1)}, u32[]{:S(2)}, u32[]{:S(2)}) collective-permute-start(f32[2,4,40,512]{3,2,1,0:T(8,128)S(1)} %get-tuple-element.48), channel_id=1, source_target_pairs={{1,0},{2,1},{3,2},{5,4},{6,5},{7,6},{9,8},{10,9},{11,10},{13,12},{... | collective-permute-start | bytes 1966088 | tf_op jit(solution)/shard_map/ppermute | solution.py:27
  79.8 1.3 collective-permute-start.10
  81.7 8.7 %all-to-all-start = ((f32[4,40,128]{2,1,0:T(8,128)}), f32[4,40,128]{2,1,0:T(8,128)S(1)}, u32[]{:S(2)}, u32[]{:S(2)}) async-start(f32[4,40,128]{2,1,0:T(8,128)} %broadcast_in_dim.158), calls=%async_computation | async-start | bytes 163840 | tf_op jit(solution)/shard_map/all_to_all | solution.py:180
  91.2 21.9 %all-to-all-done = f32[4,40,128]{2,1,0:T(8,128)S(1)} async-done(((f32[4,40,128]{2,1,0:T(8,128)}), f32[4,40,128]{2,1,0:T(8,128)S(1)}, u32[]{:S(2)}, u32[]{:S(2)}) %all-to-all-start) | async-done | bytes 81952 | tf_op jit(solution)/shard_map/all_to_all | solution.py:180
  113.4 1.6 pad_maximum_fusion.2
  116.0 2.1 fusion.51
  118.7 2.4 fusion.81
  121.8 1.7 fusion.97
  124.3 2.5 %select_reduce_fusion = (f32[32,512]{1,0:T(8,128)}, f32[8,32,512]{2,1,0:T(8,128)}) fusion(s32[32,512]{1,0:T(8,128)S(1)} %copy-done.25, s32[8]{0:T(128)S(1)} %copy-done.37, f32[14,38,512]{2,1,0:T(8,128)S(1)} %get-tuple-element.12, f32[10,34,512]{2,1,0:T(8,128)S(1)} %fusion.97, f32[14,38,512]{2,1,0:T(8,128)S(1)} %get-tuple-element.18, ...), kind=kLoop, calls=%fused_computation.237 | loop fusion | flops 2211840 | bytes 7993632 | tf_op jit(solution)/shard_map/reduce_sum | solution.py:161
  126.8 1.5 reshape.140
  129.1 7.0 %all_to_all.15 = f32[4,32,128]{2,1,0:T(8,128)} all-to-all(f32[4,32,128]{2,1,0:T(8,128)S(1)} %copy.10), channel_id=1, replica_groups=mesh['row'=8,'col'=4] {'col'}, dimensions={0} | all-to-all | bytes 131072 | tf_op jit(solution)/shard_map/all_to_all | solution.py:163
  137.6 1.9 fusion.69
  139.7 1.0 copy-done.13
  140.7 1.9 collective-permute-start.13
  142.6 2.4 collective-permute-start.12
  145.1 3.0 %collective-permute-done.12 = f32[3,4,1024]{2,1,0:T(4,128)S(1)} collective-permute-done((f32[3,4,1024]{2,1,0:T(4,128)S(1)}, f32[3,4,1024]{2,1,0:T(4,128)S(1)}, u32[]{:S(2)}, u32[]{:S(2)}) %collective-permute-start.12) | collective-permute-done | bytes 49184 | tf_op jit(solution)/shard_map/ppermute | solution.py:24
  148.8 1.7 copy-done.12
  150.6 1.3 collective-permute-start.14
  151.9 5.3 %collective-permute-start.15 = (f32[3,264,4]{2,1,0:T(8,128)S(1)}, f32[3,264,4]{2,1,0:T(8,128)}, u32[]{:S(2)}, u32[]{:S(2)}) collective-permute-start(f32[3,264,4]{2,1,0:T(8,128)S(1)} %get-tuple-element.33), channel_id=1, source_target_pairs={{1,0},{2,1},{3,2},{5,4},{6,5},{7,6},{9,8},{10,9},{11,10},{13,12},{... | collective-permute-start | bytes 38024 | tf_op jit(solution)/shard_map/ppermute | solution.py:27
  157.2 1.7 fusion.163
  158.9 1.9 collective-permute-start.19
  160.8 2.4 collective-permute-start.18
  163.2 1.7 collective-permute-done.14
  164.9 5.2 %concatenate.103 = f32[3,264,1032]{2,1,0:T(8,128)} concatenate(f32[3,264,4]{2,1,0:T(8,128)} %collective-permute-done.14, f32[3,264,1024]{2,1,0:T(8,128)} %copy-done.12, f32[3,264,4]{2,1,0:T(8,128)} %collective-permute-done.15), dimensions={2} | concatenate | bytes 6538752 | tf_op jit(solution)/shard_map/concatenate | solution.py:28
  170.1 2.4 slice_bitcast_fusion.2
  172.6 3.7 %fusion.14 = (f32[262,1030]{1,0:T(8,128)S(1)}, f32[262,1030]{1,0:T(8,128)S(1)}, f32[262,1030]{1,0:T(8,128)S(1)}, f32[262,1030]{1,0:T(8,128)S(1)}, f32[262,1030]{1,0:T(8,128)S(1)}) fusion(f32[264,1032]{1,0:T(8,128)S(1)} %get-tuple-element.27, f32[264,1032]{1,0:T(8,128)S(1)} %get-tuple-element.29, pred[264,1032]{1,0:T(8,128)(4,1)S(1)} %copy-done.9, ...), kind=kLoop, calls=%fused_computation.35 | loop fusion | flops 5936920 | bytes 17540900 | tf_op jit(solution)/shard_map/jit(_where)/select_n | solution.py:77
  177.0 4.5 %fusion.7 = f32[260,1028]{1,0:T(8,128)S(1)} fusion(f32[262,1030]{1,0:T(8,128)S(1)} %add_add_fusion, f32[262,1030]{1,0:T(8,128)S(1)} %get-tuple-element.4, f32[262,1030]{1,0:T(8,128)S(1)} %get-tuple-element.8, f32[262,1030]{1,0:T(8,128)S(1)} %get-tuple-element.7, f32[262,1030]{1,0:T(8,128)S(1)} %get-tuple-element.5, f32[262,1030]{1,0:T(8,128)S(1)} %get-tuple-element.6, ...), kind=kLoop, calls=%fused_computation.23 | loop fusion | flops 2672800 | bytes 12027600 | tf_op jit(solution)/shard_map/jit(_where)/select_n | solution.py:77
  181.5 4.7 %fusion.2 = f32[258,1026]{1,0:T(8,128)S(1)} fusion(f32[262,1030]{1,0:T(8,128)S(1)} %add_add_fusion, f32[260,1028]{1,0:T(8,128)S(1)} %fusion.7, f32[262,1030]{1,0:T(8,128)S(1)} %get-tuple-element.8, f32[262,1030]{1,0:T(8,128)S(1)} %get-tuple-element.7, f32[262,1030]{1,0:T(8,128)S(1)} %get-tuple-element.5, f32[262,1030]{1,0:T(8,128)S(1)} %get-tuple-element.6, ...), kind=kLoop, calls=%fused_computation.13 | loop fusion | flops 2647080 | bytes 11911860 | tf_op jit(solution)/shard_map/jit(_where)/select_n | solution.py:77
  186.2 4.4 %fusion.57 = (f32[32,1024]{1,0:T(8,128)S(1)}, f32[256,1024]{1,0:T(8,128)}) fusion(f32[264,1032]{1,0:T(8,128)S(1)} %get-tuple-element.28, f32[264,1032]{1,0:T(8,128)S(1)} %get-tuple-element.29, f32[262,1030]{1,0:T(8,128)S(1)} %add_add_fusion, f32[258,1026]{1,0:T(8,128)S(1)} %fusion.2, f32[262,1030]{1,0:T(8,128)S(1)} %get-tuple-element.8, ...), kind=kLoop, calls=%fused_computation.122 | loop fusion | flops 4161536 | bytes 12976128 | tf_op jit(solution)/shard_map/reduce_sum | solution.py:47
  191.0 1.9 collective-permute-start.17
  192.9 2.4 collective-permute-start.16
  195.4 1.9 pad_maximum_fusion.5
  198.5 13.4 %all-to-all-start.2 = ((f32[4,40,128]{2,1,0:T(8,128)}), f32[4,40,128]{2,1,0:T(8,128)}, u32[]{:S(2)}, u32[]{:S(2)}) async-start(f32[4,40,128]{2,1,0:T(8,128)} %broadcast_in_dim.173), calls=%async_computation.2 | async-start | bytes 163840 | tf_op jit(solution)/shard_map/all_to_all | solution.py:180
  211.9 2.0 fusion.162
  213.8 3.2 %collective-permute-start.21 = (f32[4,40,512]{2,1,0:T(8,128)}, f32[4,40,512]{2,1,0:T(8,128)}, u32[]{:S(2)}, u32[]{:S(2)}) collective-permute-start(f32[4,40,512]{2,1,0:T(8,128)} %get-tuple-element.64), channel_id=1, source_target_pairs={{1,0},{2,1},{3,2},{5,4},{6,5},{7,6},{9,8},{10,9},{11,10},{13,12},{... | collective-permute-start | bytes 983048 | tf_op jit(solution)/shard_map/ppermute | solution.py:27
  217.0 1.3 collective-permute-start.20
  219.6 3.3 %collective-permute-done.21 = f32[4,40,512]{2,1,0:T(8,128)} collective-permute-done((f32[4,40,512]{2,1,0:T(8,128)}, f32[4,40,512]{2,1,0:T(8,128)}, u32[]{:S(2)}, u32[]{:S(2)}) %collective-permute-start.21) | collective-permute-done | bytes 327712 | tf_op jit(solution)/shard_map/ppermute | solution.py:27
  222.9 8.9 %collective-permute-done.20 = f32[4,40,512]{2,1,0:T(8,128)} collective-permute-done((f32[4,40,512]{2,1,0:T(8,128)}, f32[4,40,512]{2,1,0:T(8,128)}, u32[]{:S(2)}, u32[]{:S(2)}) %collective-permute-start.20) | collective-permute-done | bytes 327712 | tf_op jit(solution)/shard_map/ppermute | solution.py:24
  231.8 1.3 pad_maximum_fusion.4
  235.5 2.0 fusion.39
  238.1 2.4 fusion.73
  240.9 1.8 fusion.89
  243.2 1.9 fusion.105
  (143 shorter events, 24.1 us)
Async XLA Ops:
  0.6 2.3 copy-start.16
  2.9 1.0 copy-start.14
  2.9 1.3 copy-start.15
  2.9 12.1 %copy-start.20 = (f32[8,32,512]{2,1,0:T(8,128)S(1)}, f32[8,32,512]{2,1,0:T(8,128)}, u32[]{:S(2)}) copy-start(f32[8,32,512]{2,1,0:T(8,128)} %param.13) | copy-start | bytes 1572868
  2.9 12.1 %copy-start.22 = (f32[8,32,512]{2,1,0:T(8,128)S(1)}, f32[8,32,512]{2,1,0:T(8,128)}, u32[]{:S(2)}) copy-start(f32[8,32,512]{2,1,0:T(8,128)} %param.12) | copy-start | bytes 1572868
  4.2 19.9 %collective-permute-start.1 = (f32[3,4,1024]{2,1,0:T(4,128)S(1)}, f32[3,4,1024]{2,1,0:T(4,128)S(1)}, u32[]{:S(2)}, u32[]{:S(2)}) collective-permute-start(f32[3,4,1024]{2,1,0:T(4,128)S(1)} %get-tuple-element.40), channel_id=1, source_target_pairs={{4,0},{8,4},{12,8},{16,12},{20,16},{24,20},{28,24},{5,1},{9,5},{13... | collective-permute-start | bytes 147464 | tf_op jit(solution)/shard_map/ppermute | solution.py:27
  6.2 18.6 %collective-permute-start = (f32[3,4,1024]{2,1,0:T(4,128)S(1)}, f32[3,4,1024]{2,1,0:T(4,128)}, u32[]{:S(2)}, u32[]{:S(2)}) collective-permute-start(f32[3,4,1024]{2,1,0:T(4,128)S(1)} %get-tuple-element.39), channel_id=1, source_target_pairs={{0,4},{4,8},{8,12},{12,16},{16,20},{20,24},{24,28},{1,5},{5,9},{9,... | collective-permute-start | bytes 147464 | tf_op jit(solution)/shard_map/ppermute | solution.py:24
  9.9 80.5 %collective-permute-start.5 = (s32[4,512]{1,0:T(4,128)}, s32[4,512]{1,0:T(4,128)}, u32[]{:S(2)}, u32[]{:S(2)}) collective-permute-start(s32[4,512]{1,0:T(4,128)} %get-tuple-element.68), channel_id=1, source_target_pairs={{4,0},{8,4},{12,8},{16,12},{20,16},{24,20},{28,24},{5,1},{9,5},{13... | collective-permute-start | bytes 24584 | tf_op jit(solution)/shard_map/ppermute | solution.py:27
  13.1 77.4 %collective-permute-start.4 = (s32[4,512]{1,0:T(4,128)}, s32[4,512]{1,0:T(4,128)}, u32[]{:S(2)}, u32[]{:S(2)}) collective-permute-start(s32[4,512]{1,0:T(4,128)} %get-tuple-element.67), channel_id=1, source_target_pairs={{0,4},{4,8},{8,12},{12,16},{16,20},{20,24},{24,28},{1,5},{5,9},{9,... | collective-permute-start | bytes 24584 | tf_op jit(solution)/shard_map/ppermute | solution.py:24
  15.8 54.8 %collective-permute-start.9 = (f32[2,8,4,512]{3,2,1,0:T(4,128)}, f32[2,8,4,512]{3,2,1,0:T(4,128)}, u32[]{:S(2)}, u32[]{:S(2)}) collective-permute-start(f32[2,8,4,512]{3,2,1,0:T(4,128)} %get-tuple-element.54), channel_id=1, source_target_pairs={{4,0},{8,4},{12,8},{16,12},{20,16},{24,20},{28,24},{5,1},{9,5},{13... | collective-permute-start | bytes 393224 | tf_op jit(solution)/shard_map/ppermute | solution.py:27
  23.5 38.2 %copy-start.8 = (pred[264,1032]{1,0:T(8,128)(4,1)}, pred[264,1032]{1,0:T(8,128)(4,1)S(1)}, u32[]{:S(2)}) copy-start(pred[264,1032]{1,0:T(8,128)(4,1)S(1)} %broadcast_and_fusion) | copy-start | bytes 817348
  24.1 0.6 copy-start.26
  27.2 14.3 %collective-permute-start.2 = (f32[3,264,4]{2,1,0:T(8,128)S(1)}, f32[3,264,4]{2,1,0:T(8,128)}, u32[]{:S(2)}, u32[]{:S(2)}) collective-permute-start(f32[3,264,4]{2,1,0:T(8,128)S(1)} %get-tuple-element.36), channel_id=1, source_target_pairs={{0,1},{1,2},{2,3},{4,5},{5,6},{6,7},{8,9},{9,10},{10,11},{12,13},{... | collective-permute-start | bytes 38024 | tf_op jit(solution)/shard_map/ppermute | solution.py:24
  28.5 14.9 %collective-permute-start.3 = (f32[3,264,4]{2,1,0:T(8,128)S(1)}, f32[3,264,4]{2,1,0:T(8,128)}, u32[]{:S(2)}, u32[]{:S(2)}) collective-permute-start(f32[3,264,4]{2,1,0:T(8,128)S(1)} %get-tuple-element.35), channel_id=1, source_target_pairs={{1,0},{2,1},{3,2},{5,4},{6,5},{7,6},{9,8},{10,9},{11,10},{13,12},{... | collective-permute-start | bytes 38024 | tf_op jit(solution)/shard_map/ppermute | solution.py:27
  41.5 31.0 %collective-permute-start.8 = (f32[2,8,4,512]{3,2,1,0:T(4,128)}, f32[2,8,4,512]{3,2,1,0:T(4,128)}, u32[]{:S(2)}, u32[]{:S(2)}) collective-permute-start(f32[2,8,4,512]{3,2,1,0:T(4,128)} %get-tuple-element.53), channel_id=1, source_target_pairs={{0,4},{4,8},{8,12},{12,16},{16,20},{20,24},{24,28},{1,5},{5,9},{9,... | collective-permute-start | bytes 393224 | tf_op jit(solution)/shard_map/ppermute | solution.py:24
  50.3 2.4 copy-start.10
  61.7 10.8 %copy-start.21 = (f32[8,32,512]{2,1,0:T(8,128)S(1)}, f32[8,32,512]{2,1,0:T(8,128)}, u32[]{:S(2)}) copy-start(f32[8,32,512]{2,1,0:T(8,128)} %param.13) | copy-start | bytes 1572868
  61.7 10.8 %copy-start.23 = (f32[8,32,512]{2,1,0:T(8,128)S(1)}, f32[8,32,512]{2,1,0:T(8,128)}, u32[]{:S(2)}) copy-start(f32[8,32,512]{2,1,0:T(8,128)} %param.12) | copy-start | bytes 1572868
  66.9 12.9 %collective-permute-start.7 = (f32[4,128]{1,0:T(4,128)S(1)}, f32[4,128]{1,0:T(4,128)S(1)}, u32[]{:S(2)}, u32[]{:S(2)}) collective-permute-start(f32[4,128]{1,0:T(4,128)S(1)} %get-tuple-element.72), channel_id=1, source_target_pairs={{4,0},{8,4},{12,8},{16,12},{20,16},{24,20},{28,24},{5,1},{9,5},{13... | collective-permute-start | bytes 6152 | tf_op jit(solution)/shard_map/ppermute | solution.py:27
  70.6 10.5 %collective-permute-start.6 = (f32[4,128]{1,0:T(4,128)S(1)}, f32[4,128]{1,0:T(4,128)S(1)}, u32[]{:S(2)}, u32[]{:S(2)}) collective-permute-start(f32[4,128]{1,0:T(4,128)S(1)} %get-tuple-element.71), channel_id=1, source_target_pairs={{0,4},{4,8},{8,12},{12,16},{16,20},{20,24},{24,28},{1,5},{5,9},{9,... | collective-permute-start | bytes 6152 | tf_op jit(solution)/shard_map/ppermute | solution.py:24
  73.7 16.8 %copy-start.24 = (s32[32,512]{1,0:T(8,128)S(1)}, s32[32,512]{1,0:T(8,128)}, u32[]{:S(2)}) copy-start(s32[32,512]{1,0:T(8,128)} %param.11) | copy-start | bytes 196612
  73.7 39.4 %copy-start.28 = (pred[16,40]{1,0:T(8,128)(4,1)S(1)}, pred[16,40]{1,0:T(8,128)(4,1)}, u32[]{:S(2)}) copy-start(pred[16,40]{1,0:T(8,128)(4,1)} %broadcast_and_fusion.1) | copy-start | bytes 1924
  73.7 39.4 %copy-start.35 = (s32[16]{0:T(128)S(1)}, s32[16]{0:T(128)}, u32[]{:S(2)}) copy-start(s32[16]{0:T(128)} %iota_add_fusion.2) | copy-start | bytes 196
  73.9 39.5 %collective-permute-start.11 = (f32[2,4,40,512]{3,2,1,0:T(8,128)S(1)}, f32[2,4,40,512]{3,2,1,0:T(8,128)S(1)}, u32[]{:S(2)}, u32[]{:S(2)}) collective-permute-start(f32[2,4,40,512]{3,2,1,0:T(8,128)S(1)} %get-tuple-element.48), channel_id=1, source_target_pairs={{1,0},{2,1},{3,2},{5,4},{6,5},{7,6},{9,8},{10,9},{11,10},{13,12},{... | collective-permute-start | bytes 1966088 | tf_op jit(solution)/shard_map/ppermute | solution.py:27
  79.8 33.6 %collective-permute-start.10 = (f32[2,4,40,512]{3,2,1,0:T(8,128)S(1)}, f32[2,4,40,512]{3,2,1,0:T(8,128)}, u32[]{:S(2)}, u32[]{:S(2)}) collective-permute-start(f32[2,4,40,512]{3,2,1,0:T(8,128)S(1)} %get-tuple-element.47), channel_id=1, source_target_pairs={{0,1},{1,2},{2,3},{4,5},{5,6},{6,7},{8,9},{9,10},{10,11},{12,13},{... | collective-permute-start | bytes 1966088 | tf_op jit(solution)/shard_map/ppermute | solution.py:24
  81.7 31.3 %all-to-all-start = ((f32[4,40,128]{2,1,0:T(8,128)}), f32[4,40,128]{2,1,0:T(8,128)S(1)}, u32[]{:S(2)}, u32[]{:S(2)}) async-start(f32[4,40,128]{2,1,0:T(8,128)} %broadcast_in_dim.158), calls=%async_computation | async-start | bytes 163840 | tf_op jit(solution)/shard_map/all_to_all | solution.py:180
  115.3 0.7 copy-start.29
  115.3 0.7 copy-start.34
  118.1 5.7 %copy-start = (f32[14,38,512]{2,1,0:T(8,128)}, f32[14,38,512]{2,1,0:T(8,128)S(1)}, u32[]{:S(2)}) copy-start(f32[14,38,512]{2,1,0:T(8,128)S(1)} %get-tuple-element.15) | copy-start | bytes 3268612
  118.1 5.7 %copy-start.2 = (f32[14,38,512]{2,1,0:T(8,128)}, f32[14,38,512]{2,1,0:T(8,128)S(1)}, u32[]{:S(2)}) copy-start(f32[14,38,512]{2,1,0:T(8,128)S(1)} %get-tuple-element.16) | copy-start | bytes 3268612
  118.1 5.7 %copy-start.4 = (f32[14,38,512]{2,1,0:T(8,128)}, f32[14,38,512]{2,1,0:T(8,128)S(1)}, u32[]{:S(2)}) copy-start(f32[14,38,512]{2,1,0:T(8,128)S(1)} %get-tuple-element.17) | copy-start | bytes 3268612
  118.1 5.7 %copy-start.6 = (f32[14,38,512]{2,1,0:T(8,128)}, f32[14,38,512]{2,1,0:T(8,128)S(1)}, u32[]{:S(2)}) copy-start(f32[14,38,512]{2,1,0:T(8,128)S(1)} %get-tuple-element.18) | copy-start | bytes 3268612
  118.1 0.6 copy-start.30
  121.1 0.7 copy-start.27
  123.5 0.8 copy-start.25
  123.5 0.8 copy-start.32
  123.5 0.8 copy-start.37
  137.6 1.9 copy-start.17
  139.5 1.2 copy-start.13
  140.7 4.3 %collective-permute-start.13 = (f32[3,4,1024]{2,1,0:T(4,128)S(1)}, f32[3,4,1024]{2,1,0:T(4,128)S(1)}, u32[]{:S(2)}, u32[]{:S(2)}) collective-permute-start(f32[3,4,1024]{2,1,0:T(4,128)S(1)} %get-tuple-element.38), channel_id=1, source_target_pairs={{4,0},{8,4},{12,8},{16,12},{20,16},{24,20},{28,24},{5,1},{9,5},{13... | collective-permute-start | bytes 147464 | tf_op jit(solution)/shard_map/ppermute | solution.py:27
  142.6 5.4 %collective-permute-start.12 = (f32[3,4,1024]{2,1,0:T(4,128)S(1)}, f32[3,4,1024]{2,1,0:T(4,128)S(1)}, u32[]{:S(2)}, u32[]{:S(2)}) collective-permute-start(f32[3,4,1024]{2,1,0:T(4,128)S(1)} %get-tuple-element.37), channel_id=1, source_target_pairs={{0,4},{4,8},{8,12},{12,16},{16,20},{20,24},{24,28},{1,5},{5,9},{9,... | collective-permute-start | bytes 147464 | tf_op jit(solution)/shard_map/ppermute | solution.py:24
  148.8 1.7 copy-start.12
  150.6 14.2 %collective-permute-start.14 = (f32[3,264,4]{2,1,0:T(8,128)S(1)}, f32[3,264,4]{2,1,0:T(8,128)}, u32[]{:S(2)}, u32[]{:S(2)}) collective-permute-start(f32[3,264,4]{2,1,0:T(8,128)S(1)} %get-tuple-element.34), channel_id=1, source_target_pairs={{0,1},{1,2},{2,3},{4,5},{5,6},{6,7},{8,9},{9,10},{10,11},{12,13},{... | collective-permute-start | bytes 38024 | tf_op jit(solution)/shard_map/ppermute | solution.py:24
  151.9 13.0 %collective-permute-start.15 = (f32[3,264,4]{2,1,0:T(8,128)S(1)}, f32[3,264,4]{2,1,0:T(8,128)}, u32[]{:S(2)}, u32[]{:S(2)}) collective-permute-start(f32[3,264,4]{2,1,0:T(8,128)S(1)} %get-tuple-element.33), channel_id=1, source_target_pairs={{1,0},{2,1},{3,2},{5,4},{6,5},{7,6},{9,8},{10,9},{11,10},{13,12},{... | collective-permute-start | bytes 38024 | tf_op jit(solution)/shard_map/ppermute | solution.py:27
  158.9 36.5 %collective-permute-start.19 = (f32[8,4,512]{2,1,0:T(4,128)}, f32[8,4,512]{2,1,0:T(4,128)}, u32[]{:S(2)}, u32[]{:S(2)}) collective-permute-start(f32[8,4,512]{2,1,0:T(4,128)} %get-tuple-element.66), channel_id=1, source_target_pairs={{4,0},{8,4},{12,8},{16,12},{20,16},{24,20},{28,24},{5,1},{9,5},{13... | collective-permute-start | bytes 196616 | tf_op jit(solution)/shard_map/ppermute | solution.py:27
  160.8 34.6 %collective-permute-start.18 = (f32[8,4,512]{2,1,0:T(4,128)}, f32[8,4,512]{2,1,0:T(4,128)}, u32[]{:S(2)}, u32[]{:S(2)}) collective-permute-start(f32[8,4,512]{2,1,0:T(4,128)} %get-tuple-element.65), channel_id=1, source_target_pairs={{0,4},{4,8},{8,12},{12,16},{16,20},{20,24},{24,28},{1,5},{5,9},{9,... | collective-permute-start | bytes 196616 | tf_op jit(solution)/shard_map/ppermute | solution.py:24
  170.1 2.4 copy-start.9
  170.1 2.5 %copy-start.11 = (f32[264,1032]{1,0:T(8,128)S(1)}, f32[264,1032]{1,0:T(8,128)}, u32[]{:S(2)}) copy-start(f32[264,1032]{1,0:T(8,128)} %copy-done.10) | copy-start | bytes 3269380
  186.2 9.2 %copy-start.18 = (f32[8,32,512]{2,1,0:T(8,128)S(1)}, f32[8,32,512]{2,1,0:T(8,128)}, u32[]{:S(2)}) copy-start(f32[8,32,512]{2,1,0:T(8,128)} %get-tuple-element.10) | copy-start | bytes 1572868
  191.0 6.2 %collective-permute-start.17 = (f32[4,128]{1,0:T(4,128)S(1)}, f32[4,128]{1,0:T(4,128)S(1)}, u32[]{:S(2)}, u32[]{:S(2)}) collective-permute-start(f32[4,128]{1,0:T(4,128)S(1)} %get-tuple-element.70), channel_id=1, source_target_pairs={{4,0},{8,4},{12,8},{16,12},{20,16},{24,20},{28,24},{5,1},{9,5},{13... | collective-permute-start | bytes 6152 | tf_op jit(solution)/shard_map/ppermute | solution.py:27
  192.9 4.9 %collective-permute-start.16 = (f32[4,128]{1,0:T(4,128)S(1)}, f32[4,128]{1,0:T(4,128)S(1)}, u32[]{:S(2)}, u32[]{:S(2)}) collective-permute-start(f32[4,128]{1,0:T(4,128)S(1)} %get-tuple-element.69), channel_id=1, source_target_pairs={{0,4},{4,8},{8,12},{12,16},{16,20},{20,24},{24,28},{1,5},{5,9},{9,... | collective-permute-start | bytes 6152 | tf_op jit(solution)/shard_map/ppermute | solution.py:24
  197.2 22.1 %copy-start.36 = (s32[16]{0:T(128)S(1)}, s32[16]{0:T(128)}, u32[]{:S(2)}) copy-start(s32[16]{0:T(128)} %iota_add_fusion.2) | copy-start | bytes 196
  198.5 19.8 %all-to-all-start.2 = ((f32[4,40,128]{2,1,0:T(8,128)}), f32[4,40,128]{2,1,0:T(8,128)}, u32[]{:S(2)}, u32[]{:S(2)}) async-start(f32[4,40,128]{2,1,0:T(8,128)} %broadcast_in_dim.173), calls=%async_computation.2 | async-start | bytes 163840 | tf_op jit(solution)/shard_map/all_to_all | solution.py:180
  213.8 9.1 %collective-permute-start.21 = (f32[4,40,512]{2,1,0:T(8,128)}, f32[4,40,512]{2,1,0:T(8,128)}, u32[]{:S(2)}, u32[]{:S(2)}) collective-permute-start(f32[4,40,512]{2,1,0:T(8,128)} %get-tuple-element.64), channel_id=1, source_target_pairs={{1,0},{2,1},{3,2},{5,4},{6,5},{7,6},{9,8},{10,9},{11,10},{13,12},{... | collective-permute-start | bytes 983048 | tf_op jit(solution)/shard_map/ppermute | solution.py:27
  217.0 14.8 %collective-permute-start.20 = (f32[4,40,512]{2,1,0:T(8,128)}, f32[4,40,512]{2,1,0:T(8,128)}, u32[]{:S(2)}, u32[]{:S(2)}) collective-permute-start(f32[4,40,512]{2,1,0:T(8,128)} %get-tuple-element.63), channel_id=1, source_target_pairs={{0,1},{1,2},{2,3},{4,5},{5,6},{6,7},{8,9},{9,10},{10,11},{12,13},{... | collective-permute-start | bytes 983048 | tf_op jit(solution)/shard_map/ppermute | solution.py:24
  218.3 13.5 %copy-start.19 = (f32[8,32,512]{2,1,0:T(8,128)S(1)}, f32[8,32,512]{2,1,0:T(8,128)}, u32[]{:S(2)}) copy-start(f32[8,32,512]{2,1,0:T(8,128)} %get-tuple-element.10) | copy-start | bytes 1572868
  233.2 1.3 copy-start.1
  233.2 1.6 copy-start.3
  233.2 1.9 copy-start.5
  233.2 2.3 copy-start.7
  237.5 0.6 copy-start.31
  242.6 0.6 copy-start.33
